TPU v7x, 32 devices: a whole 2x2x4 slice. The times are simulated.
32 devices in a mesh: parts: 2 (over x), seq: 16 (over z, y, core).
Axes of the slice: x: 2, y: 2, z: 4, core: 2. Of those that a mesh axis runs over, the one named last changes fastest.
Arguments:
- queries: bfloat16 [4096, 2048], P(('parts', 'seq')), parts along dimension 0
- joined_keys_values: bfloat16 [4096, 2048], P(('parts', 'seq')), parts along dimension 0
- segment_ids: int32 [4096], P(('parts', 'seq')), parts along dimension 0, may hold values from 0 to 3, never falling along the last dimension, each value on 1 to 1024 neighbouring positions
- residual: bfloat16 [4096, 2688], P(('parts', 'seq')), parts along dimension 0, may hold values from -4 to 4
- norm_gain: float32 [2688], replicated, may hold values from 0.5 to 1.5
- out_proj: bfloat16 [2048, 2688], P('seq'), may hold values from -1 to 1
- head_weight: bfloat16 [16384, 2688], P('seq')
- next_ids: int32 [128], P('parts'), parts along dimension 0, may hold values from 0 to 16383
Outputs:
- layer_out: bfloat16 [4096, 2688], P(('parts', 'seq')), parts along dimension 0
- log_probs: float32 [128, 16384], P('parts', 'seq'), parts along dimension 0
- target_logp: float32 [128], P(('parts', 'seq')), parts along dimension 0
There are 2 independent parts, one for each index of `parts`. A program takes and returns all parts, laid end to end along the dimension named above; an argument that names none is the same for every part. Nothing has to cross between parts.
All inputs are finite; a program needn't handle non-finite values.
Results may differ from a plain program's by a relative error of at most 0.0056.
Values may be sent and summed in bfloat16 or wider, within the bound.
No kernel may reach another device: no remote copies, remote signals or barrier semaphores. Data moves between devices by JAX's collectives and lax.ppermute only.
A program may use at most 64 MiB of HBM per device.

v0:
```python
import jax
import jax.numpy as jnp
from jax import lax
from jax.sharding import PartitionSpec as P

QUERY_HEADS = 16
KEY_VALUE_HEADS = 8
HEAD_SIZE = 128
ATTENTION_SPAN = 1024
SCORE_DEV = 4
score_scale = 168.0 ** (-0.5)
masked_score = -1e30


def shifted(value, axis, steps):
    count = lax.axis_size(axis)
    leading, last = (max(0, -steps), min(count, count - steps))
    return lax.ppermute(value, axis, [(source, source + steps) for source in range(leading, last)])


def normalize(hidden, norm_gain):
    mean_square = jnp.mean(hidden * hidden, axis=1, keepdims=True)
    return (hidden * lax.rsqrt(mean_square + 1e-06) * norm_gain[None, :]).astype(jnp.bfloat16)


def local(
    queries, joined_keys_values, segment_ids, residual, norm_gain, out_proj, head_weight, next_ids
):
    token_rows = queries.shape[0]
    blocks = ATTENTION_SPAN // token_rows
    queries_per_group = QUERY_HEADS // KEY_VALUE_HEADS
    my_index = lax.axis_index("seq")
    first_row = my_index * token_rows
    rim_kv_parts = []
    rim_seg_parts = []
    for distance in range(blocks, 0, -1):
        moved_kv, moved_seg = shifted((joined_keys_values, segment_ids), "seq", distance)
        rim_kv_parts.append(moved_kv)
        rim_seg_parts.append(moved_seg)
    rim_kv = jnp.concatenate(rim_kv_parts, 0)
    rim_seg = jnp.concatenate(rim_seg_parts, 0)
    key_value_pair = jnp.concatenate([rim_kv, joined_keys_values], 0)
    key_seg = jnp.concatenate([rim_seg, segment_ids], 0)
    count_of_keys = key_value_pair.shape[0]
    query_pos = first_row + jnp.arange(token_rows, dtype=jnp.int32)
    key_pos = first_row - blocks * token_rows + jnp.arange(count_of_keys, dtype=jnp.int32)
    allowed = (segment_ids[:, None] == key_seg[None, :]) & (key_pos[None, :] >= 0)
    allowed = (
        allowed
        & (key_pos[None, :] <= query_pos[:, None])
        & (key_pos[None, :] > query_pos[:, None] - ATTENTION_SPAN)
    )
    heads_for_queries = queries.reshape(token_rows, KEY_VALUE_HEADS, queries_per_group, HEAD_SIZE)
    heads_for_keys = key_value_pair[:, : KEY_VALUE_HEADS * HEAD_SIZE].reshape(
        count_of_keys, KEY_VALUE_HEADS, HEAD_SIZE
    )
    heads_for_values = key_value_pair[:, KEY_VALUE_HEADS * HEAD_SIZE :].reshape(
        count_of_keys, KEY_VALUE_HEADS, HEAD_SIZE
    )
    scores = (
        jnp.einsum(
            "qhgd,khd->hgqk", heads_for_queries, heads_for_keys, preferred_element_type=jnp.float32
        )
        * score_scale
    )
    scores = jnp.where(allowed[None, None, :, :], scores, masked_score)
    row_max = jnp.max(scores, axis=-1, keepdims=True)
    raised = jnp.exp(scores - row_max)
    weights = (raised / jnp.sum(raised, axis=-1, keepdims=True)).astype(jnp.bfloat16)
    context = jnp.einsum(
        "hgqk,khd->qhgd", weights, heads_for_values, preferred_element_type=jnp.float32
    )
    context = context.reshape(token_rows, QUERY_HEADS * HEAD_SIZE).astype(jnp.bfloat16)
    width = residual.shape[1]
    projected = jnp.dot(
        context,
        lax.all_gather(out_proj, "seq", axis=0, tiled=True),
        preferred_element_type=jnp.float32,
    )
    hidden = residual.astype(jnp.float32) + projected
    layer_out = hidden.astype(jnp.bfloat16)
    score_count = SCORE_DEV
    stride = token_rows // score_count
    picked = hidden.reshape(score_count, stride, width)[:, stride - 1, :]
    normed = normalize(picked, norm_gain)
    logits = lax.dot_general(
        lax.all_gather(normed, "seq", axis=0, tiled=True),
        head_weight,
        (((1,), (1,)), ((), ())),
        preferred_element_type=jnp.float32,
    )
    global_max = lax.pmax(jnp.max(logits, axis=1), "seq")
    global_total = lax.psum(jnp.sum(jnp.exp(logits - global_max[:, None]), axis=1), "seq")
    log_total = global_max + jnp.log(global_total)
    log_probs = logits - log_total[:, None]
    vocab_width = head_weight.shape[0]
    local_ids = next_ids - my_index * vocab_width
    vocab_ids = jnp.arange(vocab_width, dtype=jnp.int32)
    picked_terms = jnp.sum(
        jnp.where(local_ids[:, None] == vocab_ids[None, :], log_probs, 0.0), axis=1
    )
    target_logp = lax.psum_scatter(picked_terms, "seq", scatter_dimension=0, tiled=True)
    return (layer_out, log_probs, target_logp)


def solution(mesh):
    in_specs = (
        P(("parts", "seq"), None),
        P(("parts", "seq"), None),
        P(("parts", "seq")),
        P(("parts", "seq"), None),
        P(),
        P("seq", None),
        P("seq", None),
        P("parts"),
    )
    out_specs = (P(("parts", "seq"), None), P("parts", "seq"), P(("parts", "seq")))
    return jax.shard_map(local, mesh=mesh, in_specs=in_specs, out_specs=out_specs, check_vma=False)
```

profile of v0, /device:TPU:0, one launch (start us, length us, event | category | flops | bytes accessed | tf_op | source)
XLA Modules:
  0.0 391.8 jit_solution(2573217400198368961)
XLA Ops:
  7.2 0.0 all-gather.3.cloned.1.call-start
  7.2 0.7 all-gather.3.cloned.1.call-update
  7.9 1.3 copy.26
  9.2 6.0 %collective-permute-start = (bf16[128,2048]{0,1:T(8,128)(2,1)S(1)}, bf16[128,2048]{0,1:T(8,128)(2,1)S(1)}, u32[]{:S(2)}, u32[]{:S(2)}) collective-permute-start(bf16[128,2048]{0,1:T(8,128)(2,1)S(1)} %copy.26), channel_id=1, source_target_pairs={{0,8},{1,9},{2,10},{3,11},{4,12},{5,13},{6,14},{7,15},{16,24},{17,... | collective-permute-start | bytes 1572872 | tf_op jit(solution)/shard_map/ppermute | solution.py:18
  15.2 3.6 collective-permute-start.1
  18.8 2.2 collective-permute-start.2
  21.0 1.3 collective-permute-start.3
  22.3 1.9 collective-permute-start.8
  24.3 1.2 broadcast_subtract_fusion.1
  25.4 1.4 reshape.150
  26.9 1.2 dynamic-slice
  28.8 53.5 %collective-permute-done.8 = s32[128]{0:T(128)S(1)} collective-permute-done((s32[128]{0:T(128)}, s32[128]{0:T(128)S(1)}, u32[]{:S(2)}, u32[]{:S(2)}) %collective-permute-start.8) | collective-permute-done | bytes 544 | tf_op jit(solution)/shard_map/ppermute | solution.py:18
  82.2 87.8 %collective-permute-start.9 = (s32[128]{0:T(128)}, s32[128]{0:T(128)S(1)}, u32[]{:S(2)}, u32[]{:S(2)}) collective-permute-start(s32[128]{0:T(128)} %param.10), channel_id=1, source_target_pairs={{0,7},{1,8},{2,9},{3,10},{4,11},{5,12},{6,13},{7,14},{8,15},{16,23... | collective-permute-start | bytes 1544 | tf_op jit(solution)/shard_map/ppermute | solution.py:18
  170.1 1.4 collective-permute-done.9
  171.5 1.7 collective-permute-start.10
  173.2 1.4 collective-permute-done.10
  174.6 1.3 collective-permute-start.11
  175.9 1.4 collective-permute-done.11
  177.3 8.0 %collective-permute-start.12 = (s32[128]{0:T(128)}, s32[128]{0:T(128)S(1)}, u32[]{:S(2)}, u32[]{:S(2)}) collective-permute-start(s32[128]{0:T(128)} %param.10), channel_id=1, source_target_pairs={{0,4},{1,5},{2,6},{3,7},{4,8},{5,9},{6,10},{7,11},{8,12},{9,13},{1... | collective-permute-start | bytes 1544 | tf_op jit(solution)/shard_map/ppermute | solution.py:18
  185.3 1.4 collective-permute-done.12
  186.7 3.1 collective-permute-start.13
  189.8 1.4 collective-permute-done.13
  191.2 5.1 %collective-permute-start.14 = (s32[128]{0:T(128)}, s32[128]{0:T(128)S(1)}, u32[]{:S(2)}, u32[]{:S(2)}) collective-permute-start(s32[128]{0:T(128)} %param.10), channel_id=1, source_target_pairs={{0,2},{1,3},{2,4},{3,5},{4,6},{5,7},{6,8},{7,9},{8,10},{9,11},{10,... | collective-permute-start | bytes 1544 | tf_op jit(solution)/shard_map/ppermute | solution.py:18
  196.4 1.4 collective-permute-done.14
  197.8 1.6 collective-permute-start.15
  199.4 0.9 collective-permute-done.15
  200.4 11.4 %collective-permute-start.4 = (bf16[128,2048]{0,1:T(8,128)(2,1)S(1)}, bf16[128,2048]{0,1:T(8,128)(2,1)S(1)}, u32[]{:S(2)}, u32[]{:S(2)}) collective-permute-start(bf16[128,2048]{0,1:T(8,128)(2,1)S(1)} %copy.26), channel_id=1, source_target_pairs={{0,4},{1,5},{2,6},{3,7},{4,8},{5,9},{6,10},{7,11},{8,12},{9,13},{1... | collective-permute-start | bytes 1572872 | tf_op jit(solution)/shard_map/ppermute | solution.py:18
  211.8 0.7 constant_dynamic-update-slice_fusion.10
  212.5 1.7 compare_and_fusion
  214.2 0.0 collective-permute-done
  214.2 1.9 collective-permute-start.5
  216.1 0.1 constant_dynamic-update-slice_fusion.8
  216.2 0.0 collective-permute-done.1
  216.3 2.2 collective-permute-start.6
  218.5 0.1 constant_dynamic-update-slice_fusion.7
  218.6 0.0 collective-permute-done.2
  218.6 3.6 collective-permute-start.7
  222.2 0.1 constant_dynamic-update-slice_fusion.6
  222.3 0.1 constant_dynamic-update-slice_fusion.5
  222.5 0.0 collective-permute-done.4
  222.5 0.1 constant_dynamic-update-slice_fusion.4
  222.6 2.7 collective-permute-done.5
  225.3 0.1 constant_dynamic-update-slice_fusion.3
  225.4 11.1 %collective-permute-done.6 = bf16[128,2048]{0,1:T(8,128)(2,1)S(1)} collective-permute-done((bf16[128,2048]{0,1:T(8,128)(2,1)S(1)}, bf16[128,2048]{0,1:T(8,128)(2,1)S(1)}, u32[]{:S(2)}, u32[]{:S(2)}) %collective-permute-start.6) | collective-permute-done | bytes 524320 | tf_op jit(solution)/shard_map/ppermute | solution.py:18
  236.5 0.1 constant_dynamic-update-slice_fusion.2
  236.6 0.1 constant_dynamic-update-slice_fusion.1
  236.8 0.1 constant_dynamic-update-slice_fusion
  236.9 1.8 fusion.27
  238.7 4.2 %fusion.28 = f32[8,2,128]{2,1,0:T(2,128)} fusion(pred[128,1152]{0,1:T(8,128)(4,1)S(1)} %compare_and_fusion, bf16[1152,8,128,1]{0,2,3,1:T(8,128)(2,1)S(1)} %bitcast.43, bf16[128,8,2,128]{3,2,1,0:T(2,128)(2,1)S(1)} %reshape.150), kind=kOutput, calls=%fused_computation.55 | convolution fusion | flops 613418112 | bytes 3039232 | tf_op jit(solution)/shard_map/sub | solution.py:68
  243.0 6.3 %fusion.6 = bf16[8,128,2,128]{3,1,2,0:T(8,128)(2,1)S(1)} fusion(bf16[1152,8,128,1]{0,2,3,1:T(8,128)(2,1)} %bitcast.45, f32[8,2,128]{2,1,0:T(2,128)} %fusion.28, pred[128,1152]{0,1:T(8,128)(4,1)S(1)} %compare_and_fusion, bf16[1152,8,128,1]{0,2,3,1:T(8,128)(2,1)S(1)} %bitcast.44, bf16[128,8,2,128]{3,2,1,0:T(2,128)(2,1)S(1)} %reshape.150), kind=kOutput, calls=%fused_computation.10 | convolution fusion | flops 1220021376 | bytes 5922816 | tf_op jit(solution)/shard_map/hgqk,khd->qhgd/dot_general | solution.py:70
  249.3 0.0 all-gather.3.cloned.1.call-done
  249.3 0.0 copy-start
  249.3 6.8 %fusion.31 = (bf16[128,2688]{1,0:T(8,128)(2,1)}, f32[128,2688]{1,0:T(8,128)S(1)}) fusion(bf16[128,2048]{0,1:T(8,128)(2,1)S(1)} %bitcast.47, bf16[2048,2688]{1,0:T(8,128)(2,1)} %all-gather.3.cloned.1.call-done, bf16[128,2688]{1,0:T(8,128)(2,1)} %param.11), kind=kOutput, calls=%fused_computation.56 | convolution fusion | flops 1410318336 | bytes 14286848 | tf_op jit(solution)/shard_map/dot_general | solution.py:75
  256.2 0.1 multiply_reduce_fusion
  256.3 0.1 fusion.19
  256.4 31.9 %all-gather = bf16[16,4,2688]{2,1,0:T(4,128)(2,1)S(1)} all-gather(bf16[1,4,2688]{2,1,0:T(4,128)(2,1)S(1)} %fusion.19), channel_id=1, replica_groups=mesh['parts'=2,'seq'=16] {'seq'}, dimensions={0}, use_global_device_ids=true | all-gather | bytes 365568 | tf_op jit(solution)/shard_map/all_gather | solution.py:87
  288.3 0.1 reshape.153
  288.4 4.4 %fusion.32 = (f32[64]{0:T(128)S(1)}, f32[64,1024]{1,0:T(8,128)S(1)}) fusion(bf16[64,2688]{1,0:T(8,128)(2,1)S(1)} %reshape.153, bf16[1024,2688]{1,0:T(8,128)(2,1)} %param.14), kind=kOutput, calls=%fused_computation.57 | convolution fusion | flops 352387008 | bytes 6111488 | tf_op jit(solution)/shard_map/dot_general | solution.py:86
  292.9 31.4 %pmax.7 = f32[64]{0:T(128)S(1)} all-reduce(f32[64]{0:T(128)S(1)} %get-tuple-element.9), channel_id=1, replica_groups=mesh['parts'=2,'seq'=16] {'seq'}, use_global_device_ids=true, to_apply=%region_4.5 | all-reduce | flops 64 | bytes 512 | tf_op jit(solution)/shard_map/pmax | solution.py:92
  324.3 0.2 exponential_reduce_fusion
  324.5 29.5 %psum.7 = f32[64]{0:T(128)S(1)} all-reduce(f32[64]{0:T(128)S(1)} %exponential_reduce_fusion), channel_id=1, replica_groups=mesh['parts'=2,'seq'=16] {'seq'}, use_global_device_ids=true, to_apply=%region_6.7 | all-reduce | flops 64 | bytes 512 | tf_op jit(solution)/shard_map/psum | solution.py:93
  354.0 0.9 select_reduce_fusion
  354.9 29.5 %all-reduce = f32[64]{0:T(128)S(1)} all-reduce(f32[64]{0:T(128)S(1)} %get-tuple-element.3), channel_id=2, replica_groups=mesh['parts'=2,'seq'=16] {'seq'}, use_global_device_ids=true, to_apply=%region_8.9.clone | all-reduce | flops 64 | bytes 512
  384.4 0.6 dynamic-slice.1
  (20 shorter events, 0.1 us)
Async XLA Ops:
  7.2 242.2 %all-gather.3.cloned.1.call-start = ((), (), s32[]{:S(2)}) async-start(), calls=%async_computation | async-start | bytes 11698176 | tf_op jit(solution)/shard_map/all_gather | solution.py:77
  9.2 205.0 %collective-permute-start = (bf16[128,2048]{0,1:T(8,128)(2,1)S(1)}, bf16[128,2048]{0,1:T(8,128)(2,1)S(1)}, u32[]{:S(2)}, u32[]{:S(2)}) collective-permute-start(bf16[128,2048]{0,1:T(8,128)(2,1)S(1)} %copy.26), channel_id=1, source_target_pairs={{0,8},{1,9},{2,10},{3,11},{4,12},{5,13},{6,14},{7,15},{16,24},{17,... | collective-permute-start | bytes 1572872 | tf_op jit(solution)/shard_map/ppermute | solution.py:18
  15.2 201.0 %collective-permute-start.1 = (bf16[128,2048]{0,1:T(8,128)(2,1)S(1)}, bf16[128,2048]{0,1:T(8,128)(2,1)S(1)}, u32[]{:S(2)}, u32[]{:S(2)}) collective-permute-start(bf16[128,2048]{0,1:T(8,128)(2,1)S(1)} %copy.26), channel_id=1, source_target_pairs={{0,7},{1,8},{2,9},{3,10},{4,11},{5,12},{6,13},{7,14},{8,15},{16,23... | collective-permute-start | bytes 1572872 | tf_op jit(solution)/shard_map/ppermute | solution.py:18
  18.8 199.8 %collective-permute-start.2 = (bf16[128,2048]{0,1:T(8,128)(2,1)S(1)}, bf16[128,2048]{0,1:T(8,128)(2,1)S(1)}, u32[]{:S(2)}, u32[]{:S(2)}) collective-permute-start(bf16[128,2048]{0,1:T(8,128)(2,1)S(1)} %copy.26), channel_id=1, source_target_pairs={{0,6},{1,7},{2,8},{3,9},{4,10},{5,11},{6,12},{7,13},{8,14},{9,15},... | collective-permute-start | bytes 1572872 | tf_op jit(solution)/shard_map/ppermute | solution.py:18
  21.0 201.3 %collective-permute-start.3 = (bf16[128,2048]{0,1:T(8,128)(2,1)S(1)}, bf16[128,2048]{0,1:T(8,128)(2,1)S(1)}, u32[]{:S(2)}, u32[]{:S(2)}) collective-permute-start(bf16[128,2048]{0,1:T(8,128)(2,1)S(1)} %copy.26), channel_id=1, source_target_pairs={{0,5},{1,6},{2,7},{3,8},{4,9},{5,10},{6,11},{7,12},{8,13},{9,14},{... | collective-permute-start | bytes 1572872 | tf_op jit(solution)/shard_map/ppermute | solution.py:18
  22.3 59.9 %collective-permute-start.8 = (s32[128]{0:T(128)}, s32[128]{0:T(128)S(1)}, u32[]{:S(2)}, u32[]{:S(2)}) collective-permute-start(s32[128]{0:T(128)} %param.10), channel_id=1, source_target_pairs={{0,8},{1,9},{2,10},{3,11},{4,12},{5,13},{6,14},{7,15},{16,24},{17,... | collective-permute-start | bytes 1544 | tf_op jit(solution)/shard_map/ppermute | solution.py:18
  82.2 89.3 %collective-permute-start.9 = (s32[128]{0:T(128)}, s32[128]{0:T(128)S(1)}, u32[]{:S(2)}, u32[]{:S(2)}) collective-permute-start(s32[128]{0:T(128)} %param.10), channel_id=1, source_target_pairs={{0,7},{1,8},{2,9},{3,10},{4,11},{5,12},{6,13},{7,14},{8,15},{16,23... | collective-permute-start | bytes 1544 | tf_op jit(solution)/shard_map/ppermute | solution.py:18
  171.5 3.1 collective-permute-start.10
  174.6 2.7 collective-permute-start.11
  177.3 9.5 %collective-permute-start.12 = (s32[128]{0:T(128)}, s32[128]{0:T(128)S(1)}, u32[]{:S(2)}, u32[]{:S(2)}) collective-permute-start(s32[128]{0:T(128)} %param.10), channel_id=1, source_target_pairs={{0,4},{1,5},{2,6},{3,7},{4,8},{5,9},{6,10},{7,11},{8,12},{9,13},{1... | collective-permute-start | bytes 1544 | tf_op jit(solution)/shard_map/ppermute | solution.py:18
  186.7 4.5 %collective-permute-start.13 = (s32[128]{0:T(128)}, s32[128]{0:T(128)S(1)}, u32[]{:S(2)}, u32[]{:S(2)}) collective-permute-start(s32[128]{0:T(128)} %param.10), channel_id=1, source_target_pairs={{0,3},{1,4},{2,5},{3,6},{4,7},{5,8},{6,9},{7,10},{8,11},{9,12},{10... | collective-permute-start | bytes 1544 | tf_op jit(solution)/shard_map/ppermute | solution.py:18
  191.2 6.6 %collective-permute-start.14 = (s32[128]{0:T(128)}, s32[128]{0:T(128)S(1)}, u32[]{:S(2)}, u32[]{:S(2)}) collective-permute-start(s32[128]{0:T(128)} %param.10), channel_id=1, source_target_pairs={{0,2},{1,3},{2,4},{3,5},{4,6},{5,7},{6,8},{7,9},{8,10},{9,11},{10,... | collective-permute-start | bytes 1544 | tf_op jit(solution)/shard_map/ppermute | solution.py:18
  197.8 2.6 collective-permute-start.15
  200.4 22.1 %collective-permute-start.4 = (bf16[128,2048]{0,1:T(8,128)(2,1)S(1)}, bf16[128,2048]{0,1:T(8,128)(2,1)S(1)}, u32[]{:S(2)}, u32[]{:S(2)}) collective-permute-start(bf16[128,2048]{0,1:T(8,128)(2,1)S(1)} %copy.26), channel_id=1, source_target_pairs={{0,4},{1,5},{2,6},{3,7},{4,8},{5,9},{6,10},{7,11},{8,12},{9,13},{1... | collective-permute-start | bytes 1572872 | tf_op jit(solution)/shard_map/ppermute | solution.py:18
  214.2 11.1 %collective-permute-start.5 = (bf16[128,2048]{0,1:T(8,128)(2,1)S(1)}, bf16[128,2048]{0,1:T(8,128)(2,1)S(1)}, u32[]{:S(2)}, u32[]{:S(2)}) collective-permute-start(bf16[128,2048]{0,1:T(8,128)(2,1)S(1)} %copy.26), channel_id=1, source_target_pairs={{0,3},{1,4},{2,5},{3,6},{4,7},{5,8},{6,9},{7,10},{8,11},{9,12},{10... | collective-permute-start | bytes 1572872 | tf_op jit(solution)/shard_map/ppermute | solution.py:18
  216.3 20.2 %collective-permute-start.6 = (bf16[128,2048]{0,1:T(8,128)(2,1)S(1)}, bf16[128,2048]{0,1:T(8,128)(2,1)S(1)}, u32[]{:S(2)}, u32[]{:S(2)}) collective-permute-start(bf16[128,2048]{0,1:T(8,128)(2,1)S(1)} %copy.26), channel_id=1, source_target_pairs={{0,2},{1,3},{2,4},{3,5},{4,6},{5,7},{6,8},{7,9},{8,10},{9,11},{10,... | collective-permute-start | bytes 1572872 | tf_op jit(solution)/shard_map/ppermute | solution.py:18
  218.6 18.0 %collective-permute-start.7 = (bf16[128,2048]{0,1:T(8,128)(2,1)S(1)}, bf16[128,2048]{0,1:T(8,128)(2,1)S(1)}, u32[]{:S(2)}, u32[]{:S(2)}) collective-permute-start(bf16[128,2048]{0,1:T(8,128)(2,1)S(1)} %copy.26), channel_id=1, source_target_pairs={{0,1},{1,2},{2,3},{3,4},{4,5},{5,6},{6,7},{7,8},{8,9},{9,10},{10,1... | collective-permute-start | bytes 1572872 | tf_op jit(solution)/shard_map/ppermute | solution.py:18
  249.3 7.0 %copy-start = (f32[2688]{0:T(1024)S(1)}, f32[2688]{0:T(1024)}, u32[]{:S(2)}) copy-start(f32[2688]{0:T(1024)} %param.12) | copy-start | bytes 32260
  256.1 97.9 %copy-start.1 = (s32[64]{0:T(128)S(1)}, s32[64]{0:T(128)}, u32[]{:S(2)}) copy-start(s32[64]{0:T(128)} %broadcast_subtract_fusion.1) | copy-start | bytes 772
Sparse Core Ops, SparseCore 0:
  10.3 136.2 all-gather.2
where the time goes:
time: 393 us; the launch traced here: 392 us
  starting transfers between devices  143 us (36%)
  blocking collectives  122 us (31%)
  waiting for transfers between devices  77.3 us (20%)
  matrix products  21.8 us (6%)
  between operations  15.1 us (4%)
  local copies, waits for them, and re-layouts  8.31 us (2%)
  other arithmetic  4.24 us (1%)
    ppermute x16, starting transfers between devices, shifted(): lax.ppermute(value, axis, [(source, source + steps) for source in range(l...  143 us
    ppermute x16, waiting for transfers between devices, shifted(): lax.ppermute(value, axis, [(source, source + steps) for source in range(l...  76.6 us
    all_gather x1, blocking collectives, local(): lax.all_gather(normed, 'seq', axis=0, tiled=True)  31.9 us
    pmax x1, blocking collectives, local(): global_max = lax.pmax(jnp.max(logits, axis=1), 'seq')  31.4 us
    unnamed x1, blocking collectives  29.5 us
    psum x1, blocking collectives, local(): lax.psum(jnp.sum(jnp.exp(logits - global_max[:, None]), axis=1), 'seq')  29.5 us
  transfers between devices with their start and end apart: 17, of which 10 were waited for; matrix products, arithmetic and copies ran while one was open for 5% of the time, Pallas kernels for 0%

commit v1 on v0

--- a/solution.py
+++ b/solution.py
@@ -1,7 +1,9 @@
+import functools
 import jax
 import jax.numpy as jnp
 from jax import lax
 from jax.sharding import PartitionSpec as P
+from jax.lax import axis_index, axis_size, ppermute
 
 QUERY_HEADS = 16
 KEY_VALUE_HEADS = 8
@@ -10,6 +12,25 @@
 SCORE_DEV = 4
 score_scale = 168.0 ** (-0.5)
 masked_score = -1e30
+
+
+def build_spot_up(payload, along_axis):
+    dev_count = axis_size(along_axis)
+    all_rows = list(map(lambda to_i: (to_i, (to_i + 1) % dev_count), range(dev_count)))
+    store = list(map(lambda to_i: (to_i, (to_i - 1) % dev_count), range(dev_count)))
+    v1, side_arr = ([payload], [payload])
+    for _ in range(dev_count // 2):
+        v1.append(ppermute(v1[-1], along_axis, perm=all_rows))
+    for _ in range((dev_count - 1) // 2):
+        side_arr.append(ppermute(side_arr[-1], along_axis, store))
+    return jnp.roll(
+        jnp.concatenate([*v1[::-1], *side_arr[1:]], axis=0),
+        shift=(axis_index(along_axis) - dev_count // 2) * payload.shape[0],
+        axis=0,
+    )
+
+
+trace_goods = functools.partial(build_spot_up, along_axis="seq")
 
 
 def shifted(value, axis, steps):
@@ -84,7 +105,7 @@
     picked = hidden.reshape(score_count, stride, width)[:, stride - 1, :]
     normed = normalize(picked, norm_gain)
     logits = lax.dot_general(
-        lax.all_gather(normed, "seq", axis=0, tiled=True),
+        trace_goods(normed),
         head_weight,
         (((1,), (1,)), ((), ())),
         preferred_element_type=jnp.float32,

time: 393 us -> 407 us (1.036)
  starting transfers between devices: 143 us -> 177 us
  blocking collectives: 122 us -> 88.5 us
  waiting for transfers between devices: 77.3 us -> 92.5 us
    ppermute x0 -> x15, starting transfers between devices: none -> 34.3 us  [the longest x8 18.4 us: build_spot_up(): v1.append(ppermute(v1[-1], along_axis, perm=all_rows))]
    all_gather x1 -> x0, blocking collectives: 31.9 us -> none  [local(): lax.all_gather(normed, 'seq', axis=0, tiled=True)]
    ppermute x0 -> x15, waiting for transfers between devices: none -> 12.1 us  [the longest x8 7.81 us: build_spot_up(): v1.append(ppermute(v1[-1], along_axis, perm=all_rows))]
  transfers between devices with their start and end apart: 17 -> 32, of which waited for: 10 -> 24; matrix products, arithmetic and copies ran while one was open for 5% -> 5% of each run, Pallas kernels for 0% -> 0%
where the time goes in v1:
time: 407 us; the launch traced here: 406 us
  starting transfers between devices  177 us (43%)
  waiting for transfers between devices  92.5 us (23%)
  blocking collectives  88.5 us (22%)
  matrix products  21.8 us (5%)
  between operations  15.2 us (4%)
  local copies, waits for them, and re-layouts  8.39 us (2%)
    ppermute x16, starting transfers between devices, shifted(): lax.ppermute(value, axis, [(source, source + steps) for source in range(l...  143 us
    ppermute x16, waiting for transfers between devices, shifted(): lax.ppermute(value, axis, [(source, source + steps) for source in range(l...  79.7 us
    pmax x1, blocking collectives, local(): global_max = lax.pmax(jnp.max(logits, axis=1), 'seq')  29.5 us
    unnamed x1, blocking collectives  29.5 us
    psum x1, blocking collectives, local(): lax.psum(jnp.sum(jnp.exp(logits - global_max[:, None]), axis=1), 'seq')  29.5 us
    ppermute x8, starting transfers between devices, build_spot_up(): v1.append(ppermute(v1[-1], along_axis, perm=all_rows))  18.4 us
    ppermute x7, starting transfers between devices, build_spot_up(): side_arr.append(ppermute(side_arr[-1], along_axis, store))  15.9 us
  transfers between devices with their start and end apart: 32, of which 24 were waited for; matrix products, arithmetic and copies ran while one was open for 5% of the time, Pallas kernels for 0%

profile of v1, /device:TPU:0, one launch (start us, length us, event | category | flops | bytes accessed | tf_op | source)
XLA Modules:
  0.0 406.4 jit_solution(11620603959413777650)
XLA Ops:
  7.2 0.7 all-gather.2.cloned.1.call-update
  7.9 1.3 copy.26
  9.2 6.0 %collective-permute-start = (bf16[128,2048]{0,1:T(8,128)(2,1)S(1)}, bf16[128,2048]{0,1:T(8,128)(2,1)S(1)}, u32[]{:S(2)}, u32[]{:S(2)}) collective-permute-start(bf16[128,2048]{0,1:T(8,128)(2,1)S(1)} %copy.26), channel_id=1, source_target_pairs={{0,8},{1,9},{2,10},{3,11},{4,12},{5,13},{6,14},{7,15},{16,24},{17,... | collective-permute-start | bytes 1572872 | tf_op jit(solution)/shard_map/ppermute | solution.py:39
  15.2 3.6 collective-permute-start.1
  18.8 2.2 collective-permute-start.2
  21.0 1.3 collective-permute-start.3
  22.3 1.9 collective-permute-start.8
  24.3 1.4 reshape.150
  25.7 56.6 %collective-permute-done.8 = s32[128]{0:T(128)S(1)} collective-permute-done((s32[128]{0:T(128)}, s32[128]{0:T(128)S(1)}, u32[]{:S(2)}, u32[]{:S(2)}) %collective-permute-start.8) | collective-permute-done | bytes 544 | tf_op jit(solution)/shard_map/ppermute | solution.py:39
  82.2 87.8 %collective-permute-start.9 = (s32[128]{0:T(128)}, s32[128]{0:T(128)S(1)}, u32[]{:S(2)}, u32[]{:S(2)}) collective-permute-start(s32[128]{0:T(128)} %param.10), channel_id=1, source_target_pairs={{0,7},{1,8},{2,9},{3,10},{4,11},{5,12},{6,13},{7,14},{8,15},{16,23... | collective-permute-start | bytes 1544 | tf_op jit(solution)/shard_map/ppermute | solution.py:39
  170.1 1.4 collective-permute-done.9
  171.5 1.7 collective-permute-start.10
  173.2 1.4 collective-permute-done.10
  174.6 1.3 collective-permute-start.11
  175.9 1.4 collective-permute-done.11
  177.3 8.0 %collective-permute-start.12 = (s32[128]{0:T(128)}, s32[128]{0:T(128)S(1)}, u32[]{:S(2)}, u32[]{:S(2)}) collective-permute-start(s32[128]{0:T(128)} %param.10), channel_id=1, source_target_pairs={{0,4},{1,5},{2,6},{3,7},{4,8},{5,9},{6,10},{7,11},{8,12},{9,13},{1... | collective-permute-start | bytes 1544 | tf_op jit(solution)/shard_map/ppermute | solution.py:39
  185.3 1.4 collective-permute-done.12
  186.7 3.1 collective-permute-start.13
  189.8 1.4 collective-permute-done.13
  191.2 5.1 %collective-permute-start.14 = (s32[128]{0:T(128)}, s32[128]{0:T(128)S(1)}, u32[]{:S(2)}, u32[]{:S(2)}) collective-permute-start(s32[128]{0:T(128)} %param.10), channel_id=1, source_target_pairs={{0,2},{1,3},{2,4},{3,5},{4,6},{5,7},{6,8},{7,9},{8,10},{9,11},{10,... | collective-permute-start | bytes 1544 | tf_op jit(solution)/shard_map/ppermute | solution.py:39
  196.4 1.4 collective-permute-done.14
  197.8 1.6 collective-permute-start.15
  199.4 0.9 collective-permute-done.15
  200.4 11.4 %collective-permute-start.4 = (bf16[128,2048]{0,1:T(8,128)(2,1)S(1)}, bf16[128,2048]{0,1:T(8,128)(2,1)S(1)}, u32[]{:S(2)}, u32[]{:S(2)}) collective-permute-start(bf16[128,2048]{0,1:T(8,128)(2,1)S(1)} %copy.26), channel_id=1, source_target_pairs={{0,4},{1,5},{2,6},{3,7},{4,8},{5,9},{6,10},{7,11},{8,12},{9,13},{1... | collective-permute-start | bytes 1572872 | tf_op jit(solution)/shard_map/ppermute | solution.py:39
  211.8 0.7 constant_dynamic-update-slice_fusion.10
  212.5 1.7 compare_and_fusion
  214.2 1.9 collective-permute-start.5
  216.3 2.2 collective-permute-start.6
  218.6 3.6 collective-permute-start.7
  222.6 2.7 collective-permute-done.5
  225.4 11.1 %collective-permute-done.6 = bf16[128,2048]{0,1:T(8,128)(2,1)S(1)} collective-permute-done((bf16[128,2048]{0,1:T(8,128)(2,1)S(1)}, bf16[128,2048]{0,1:T(8,128)(2,1)S(1)}, u32[]{:S(2)}, u32[]{:S(2)}) %collective-permute-start.6) | collective-permute-done | bytes 524320 | tf_op jit(solution)/shard_map/ppermute | solution.py:39
  236.9 1.9 fusion.32
  238.8 4.2 %fusion.33 = f32[8,2,128]{2,1,0:T(2,128)} fusion(pred[128,1152]{0,1:T(8,128)(4,1)S(1)} %compare_and_fusion, bf16[1152,8,128,1]{0,2,3,1:T(8,128)(2,1)S(1)} %bitcast.41, bf16[128,8,2,128]{3,2,1,0:T(2,128)(2,1)S(1)} %reshape.150), kind=kOutput, calls=%fused_computation.59 | convolution fusion | flops 613418112 | bytes 3039232 | tf_op jit(solution)/shard_map/sub | solution.py:89
  243.0 6.3 %fusion.6 = bf16[8,128,2,128]{3,1,2,0:T(8,128)(2,1)S(1)} fusion(bf16[1152,8,128,1]{0,2,3,1:T(8,128)(2,1)} %bitcast.43, f32[8,2,128]{2,1,0:T(2,128)} %fusion.33, pred[128,1152]{0,1:T(8,128)(4,1)S(1)} %compare_and_fusion, bf16[1152,8,128,1]{0,2,3,1:T(8,128)(2,1)S(1)} %bitcast.42, bf16[128,8,2,128]{3,2,1,0:T(2,128)(2,1)S(1)} %reshape.150), kind=kOutput, calls=%fused_computation.10 | convolution fusion | flops 1220021376 | bytes 5922816 | tf_op jit(solution)/shard_map/hgqk,khd->qhgd/dot_general | solution.py:91
  249.4 6.8 %fusion.36 = (bf16[128,2688]{1,0:T(8,128)(2,1)}, f32[128,2688]{1,0:T(8,128)S(1)}) fusion(bf16[128,2048]{0,1:T(8,128)(2,1)S(1)} %bitcast.45, bf16[2048,2688]{1,0:T(8,128)(2,1)} %all-gather.2.cloned.1.call-done, bf16[128,2688]{1,0:T(8,128)(2,1)} %param.11), kind=kOutput, calls=%fused_computation.60 | convolution fusion | flops 1410318336 | bytes 14286848 | tf_op jit(solution)/shard_map/dot_general | solution.py:96
  256.2 0.1 fusion.21
  256.5 3.2 collective-permute-start.16
  259.6 1.3 collective-permute-start.24
  261.0 1.5 collective-permute-done.16
  262.4 4.8 %collective-permute-start.17 = (bf16[4,2688]{1,0:T(4,128)(2,1)S(1)}, bf16[4,2688]{1,0:T(4,128)(2,1)S(1)}, u32[]{:S(2)}, u32[]{:S(2)}) collective-permute-start(bf16[4,2688]{1,0:T(4,128)(2,1)S(1)} %collective-permute-done.16), channel_id=1, source_target_pairs={{0,1},{1,2},{2,3},{3,4},{4,5},{5,6},{6,7},{7,8},{8,9},{9,10},{10,1... | collective-permute-start | bytes 64520 | tf_op jit(solution)/shard_map/ppermute | solution.py:23
  267.2 1.1 collective-permute-done.17
  268.3 5.4 %collective-permute-start.18 = (bf16[4,2688]{1,0:T(4,128)(2,1)S(1)}, bf16[4,2688]{1,0:T(4,128)(2,1)S(1)}, u32[]{:S(2)}, u32[]{:S(2)}) collective-permute-start(bf16[4,2688]{1,0:T(4,128)(2,1)S(1)} %collective-permute-done.17), channel_id=1, source_target_pairs={{0,1},{1,2},{2,3},{3,4},{4,5},{5,6},{6,7},{7,8},{8,9},{9,10},{10,1... | collective-permute-start | bytes 64520 | tf_op jit(solution)/shard_map/ppermute | solution.py:23
  273.7 0.7 collective-permute-done.25
  274.4 0.2 collective-permute-done.18
  274.6 3.4 collective-permute-start.19
  278.0 0.4 collective-permute-done.26
  278.4 2.0 collective-permute-start.27
  280.5 1.6 collective-permute-start.20
  282.1 0.4 collective-permute-done.27
  282.5 3.8 collective-permute-start.28
  286.4 1.4 collective-permute-done.28
  287.8 4.4 %collective-permute-start.29 = (bf16[4,2688]{1,0:T(4,128)(2,1)S(1)}, bf16[4,2688]{1,0:T(4,128)(2,1)S(1)}, u32[]{:S(2)}, u32[]{:S(2)}) collective-permute-start(bf16[4,2688]{1,0:T(4,128)(2,1)S(1)} %collective-permute-done.28), channel_id=1, source_target_pairs={{0,15},{1,0},{2,1},{3,2},{4,3},{5,4},{6,5},{7,6},{8,7},{9,8},{10,9... | collective-permute-start | bytes 64520 | tf_op jit(solution)/shard_map/ppermute | solution.py:25
  292.3 1.4 collective-permute-done.29
  293.7 4.4 %collective-permute-start.30 = (bf16[4,2688]{1,0:T(4,128)(2,1)S(1)}, bf16[4,2688]{1,0:T(4,128)(2,1)S(1)}, u32[]{:S(2)}, u32[]{:S(2)}) collective-permute-start(bf16[4,2688]{1,0:T(4,128)(2,1)S(1)} %collective-permute-done.29), channel_id=1, source_target_pairs={{0,15},{1,0},{2,1},{3,2},{4,3},{5,4},{6,5},{7,6},{8,7},{9,8},{10,9... | collective-permute-start | bytes 64520 | tf_op jit(solution)/shard_map/ppermute | solution.py:25
  298.3 0.6 dynamic-slice
  299.6 4.5 %collective-permute-done.23 = bf16[4,2688]{1,0:T(4,128)(2,1)S(1)} collective-permute-done((bf16[4,2688]{1,0:T(4,128)(2,1)S(1)}, bf16[4,2688]{1,0:T(4,128)(2,1)S(1)}, u32[]{:S(2)}, u32[]{:S(2)}) %collective-permute-start.23) | collective-permute-done | bytes 21536 | tf_op jit(solution)/shard_map/ppermute | solution.py:23
  304.1 0.8 concatenate.14
  304.9 4.4 %fusion.37 = (f32[64]{0:T(128)S(1)}, f32[64,1024]{1,0:T(8,128)S(1)}) fusion(bf16[1024,2688]{1,0:T(8,128)(2,1)} %param.14, bf16[128,2688]{1,0:T(8,128)(2,1)S(1)} %concatenate.14, s32[]{:T(128)S(6)} %select_n.23), kind=kOutput, calls=%fused_computation.61 | convolution fusion | flops 352387008 | bytes 6111492 | tf_op jit(solution)/shard_map/dot_general | solution.py:107
  309.4 29.5 %pmax.7 = f32[64]{0:T(128)S(1)} all-reduce(f32[64]{0:T(128)S(1)} %get-tuple-element.9), channel_id=1, replica_groups=mesh['parts'=2,'seq'=16] {'seq'}, use_global_device_ids=true, to_apply=%region_4.5 | all-reduce | flops 64 | bytes 512 | tf_op jit(solution)/shard_map/pmax | solution.py:113
  338.9 0.2 exponential_reduce_fusion
  339.1 29.5 %psum.7 = f32[64]{0:T(128)S(1)} all-reduce(f32[64]{0:T(128)S(1)} %exponential_reduce_fusion), channel_id=1, replica_groups=mesh['parts'=2,'seq'=16] {'seq'}, use_global_device_ids=true, to_apply=%region_6.7 | all-reduce | flops 64 | bytes 512 | tf_op jit(solution)/shard_map/psum | solution.py:114
  368.6 0.9 select_reduce_fusion
  369.5 29.5 %all-reduce = f32[64]{0:T(128)S(1)} all-reduce(f32[64]{0:T(128)S(1)} %get-tuple-element.3), channel_id=2, replica_groups=mesh['parts'=2,'seq'=16] {'seq'}, use_global_device_ids=true, to_apply=%region_8.9.clone | all-reduce | flops 64 | bytes 512
  399.0 0.6 dynamic-slice.1
  (51 shorter events, 2.0 us)
Async XLA Ops:
  7.2 242.2 %all-gather.2.cloned.1.call-start = ((), (), s32[]{:S(2)}) async-start(), calls=%async_computation | async-start | bytes 11698176 | tf_op jit(solution)/shard_map/all_gather | solution.py:98
  9.2 205.0 %collective-permute-start = (bf16[128,2048]{0,1:T(8,128)(2,1)S(1)}, bf16[128,2048]{0,1:T(8,128)(2,1)S(1)}, u32[]{:S(2)}, u32[]{:S(2)}) collective-permute-start(bf16[128,2048]{0,1:T(8,128)(2,1)S(1)} %copy.26), channel_id=1, source_target_pairs={{0,8},{1,9},{2,10},{3,11},{4,12},{5,13},{6,14},{7,15},{16,24},{17,... | collective-permute-start | bytes 1572872 | tf_op jit(solution)/shard_map/ppermute | solution.py:39
  15.2 201.0 %collective-permute-start.1 = (bf16[128,2048]{0,1:T(8,128)(2,1)S(1)}, bf16[128,2048]{0,1:T(8,128)(2,1)S(1)}, u32[]{:S(2)}, u32[]{:S(2)}) collective-permute-start(bf16[128,2048]{0,1:T(8,128)(2,1)S(1)} %copy.26), channel_id=1, source_target_pairs={{0,7},{1,8},{2,9},{3,10},{4,11},{5,12},{6,13},{7,14},{8,15},{16,23... | collective-permute-start | bytes 1572872 | tf_op jit(solution)/shard_map/ppermute | solution.py:39
  18.8 199.8 %collective-permute-start.2 = (bf16[128,2048]{0,1:T(8,128)(2,1)S(1)}, bf16[128,2048]{0,1:T(8,128)(2,1)S(1)}, u32[]{:S(2)}, u32[]{:S(2)}) collective-permute-start(bf16[128,2048]{0,1:T(8,128)(2,1)S(1)} %copy.26), channel_id=1, source_target_pairs={{0,6},{1,7},{2,8},{3,9},{4,10},{5,11},{6,12},{7,13},{8,14},{9,15},... | collective-permute-start | bytes 1572872 | tf_op jit(solution)/shard_map/ppermute | solution.py:39
  21.0 201.3 %collective-permute-start.3 = (bf16[128,2048]{0,1:T(8,128)(2,1)S(1)}, bf16[128,2048]{0,1:T(8,128)(2,1)S(1)}, u32[]{:S(2)}, u32[]{:S(2)}) collective-permute-start(bf16[128,2048]{0,1:T(8,128)(2,1)S(1)} %copy.26), channel_id=1, source_target_pairs={{0,5},{1,6},{2,7},{3,8},{4,9},{5,10},{6,11},{7,12},{8,13},{9,14},{... | collective-permute-start | bytes 1572872 | tf_op jit(solution)/shard_map/ppermute | solution.py:39
  22.3 59.9 %collective-permute-start.8 = (s32[128]{0:T(128)}, s32[128]{0:T(128)S(1)}, u32[]{:S(2)}, u32[]{:S(2)}) collective-permute-start(s32[128]{0:T(128)} %param.10), channel_id=1, source_target_pairs={{0,8},{1,9},{2,10},{3,11},{4,12},{5,13},{6,14},{7,15},{16,24},{17,... | collective-permute-start | bytes 1544 | tf_op jit(solution)/shard_map/ppermute | solution.py:39
  82.2 89.3 %collective-permute-start.9 = (s32[128]{0:T(128)}, s32[128]{0:T(128)S(1)}, u32[]{:S(2)}, u32[]{:S(2)}) collective-permute-start(s32[128]{0:T(128)} %param.10), channel_id=1, source_target_pairs={{0,7},{1,8},{2,9},{3,10},{4,11},{5,12},{6,13},{7,14},{8,15},{16,23... | collective-permute-start | bytes 1544 | tf_op jit(solution)/shard_map/ppermute | solution.py:39
  171.5 3.1 collective-permute-start.10
  174.6 2.7 collective-permute-start.11
  177.3 9.5 %collective-permute-start.12 = (s32[128]{0:T(128)}, s32[128]{0:T(128)S(1)}, u32[]{:S(2)}, u32[]{:S(2)}) collective-permute-start(s32[128]{0:T(128)} %param.10), channel_id=1, source_target_pairs={{0,4},{1,5},{2,6},{3,7},{4,8},{5,9},{6,10},{7,11},{8,12},{9,13},{1... | collective-permute-start | bytes 1544 | tf_op jit(solution)/shard_map/ppermute | solution.py:39
  186.7 4.5 %collective-permute-start.13 = (s32[128]{0:T(128)}, s32[128]{0:T(128)S(1)}, u32[]{:S(2)}, u32[]{:S(2)}) collective-permute-start(s32[128]{0:T(128)} %param.10), channel_id=1, source_target_pairs={{0,3},{1,4},{2,5},{3,6},{4,7},{5,8},{6,9},{7,10},{8,11},{9,12},{10... | collective-permute-start | bytes 1544 | tf_op jit(solution)/shard_map/ppermute | solution.py:39
  191.2 6.6 %collective-permute-start.14 = (s32[128]{0:T(128)}, s32[128]{0:T(128)S(1)}, u32[]{:S(2)}, u32[]{:S(2)}) collective-permute-start(s32[128]{0:T(128)} %param.10), channel_id=1, source_target_pairs={{0,2},{1,3},{2,4},{3,5},{4,6},{5,7},{6,8},{7,9},{8,10},{9,11},{10,... | collective-permute-start | bytes 1544 | tf_op jit(solution)/shard_map/ppermute | solution.py:39
  197.8 2.6 collective-permute-start.15
  200.4 22.1 %collective-permute-start.4 = (bf16[128,2048]{0,1:T(8,128)(2,1)S(1)}, bf16[128,2048]{0,1:T(8,128)(2,1)S(1)}, u32[]{:S(2)}, u32[]{:S(2)}) collective-permute-start(bf16[128,2048]{0,1:T(8,128)(2,1)S(1)} %copy.26), channel_id=1, source_target_pairs={{0,4},{1,5},{2,6},{3,7},{4,8},{5,9},{6,10},{7,11},{8,12},{9,13},{1... | collective-permute-start | bytes 1572872 | tf_op jit(solution)/shard_map/ppermute | solution.py:39
  214.2 11.1 %collective-permute-start.5 = (bf16[128,2048]{0,1:T(8,128)(2,1)S(1)}, bf16[128,2048]{0,1:T(8,128)(2,1)S(1)}, u32[]{:S(2)}, u32[]{:S(2)}) collective-permute-start(bf16[128,2048]{0,1:T(8,128)(2,1)S(1)} %copy.26), channel_id=1, source_target_pairs={{0,3},{1,4},{2,5},{3,6},{4,7},{5,8},{6,9},{7,10},{8,11},{9,12},{10... | collective-permute-start | bytes 1572872 | tf_op jit(solution)/shard_map/ppermute | solution.py:39
  216.3 20.2 %collective-permute-start.6 = (bf16[128,2048]{0,1:T(8,128)(2,1)S(1)}, bf16[128,2048]{0,1:T(8,128)(2,1)S(1)}, u32[]{:S(2)}, u32[]{:S(2)}) collective-permute-start(bf16[128,2048]{0,1:T(8,128)(2,1)S(1)} %copy.26), channel_id=1, source_target_pairs={{0,2},{1,3},{2,4},{3,5},{4,6},{5,7},{6,8},{7,9},{8,10},{9,11},{10,... | collective-permute-start | bytes 1572872 | tf_op jit(solution)/shard_map/ppermute | solution.py:39
  218.6 18.0 %collective-permute-start.7 = (bf16[128,2048]{0,1:T(8,128)(2,1)S(1)}, bf16[128,2048]{0,1:T(8,128)(2,1)S(1)}, u32[]{:S(2)}, u32[]{:S(2)}) collective-permute-start(bf16[128,2048]{0,1:T(8,128)(2,1)S(1)} %copy.26), channel_id=1, source_target_pairs={{0,1},{1,2},{2,3},{3,4},{4,5},{5,6},{6,7},{7,8},{8,9},{9,10},{10,1... | collective-permute-start | bytes 1572872 | tf_op jit(solution)/shard_map/ppermute | solution.py:39
  249.4 7.0 %copy-start = (f32[2688]{0:T(1024)S(1)}, f32[2688]{0:T(1024)}, u32[]{:S(2)}) copy-start(f32[2688]{0:T(1024)} %param.12) | copy-start | bytes 32260
  249.4 48.9 %copy-start.1 = (s32[64]{0:T(128)S(1)}, s32[64]{0:T(128)}, u32[]{:S(2)}) copy-start(s32[64]{0:T(128)} %param.15) | copy-start | bytes 772
  249.4 48.9 %copy-start.2 = (u32[32]{0:T(128)S(1)}, u32[32]{0:T(128)}, u32[]{:S(2)}) copy-start(u32[32]{0:T(128)} %constant.55) | copy-start | bytes 388
  256.5 6.0 %collective-permute-start.16 = (bf16[4,2688]{1,0:T(4,128)(2,1)S(1)}, bf16[4,2688]{1,0:T(4,128)(2,1)S(1)}, u32[]{:S(2)}, u32[]{:S(2)}) collective-permute-start(bf16[4,2688]{1,0:T(4,128)(2,1)S(1)} %fusion.23), channel_id=1, source_target_pairs={{0,1},{1,2},{2,3},{3,4},{4,5},{5,6},{6,7},{7,8},{8,9},{9,10},{10,1... | collective-permute-start | bytes 64520 | tf_op jit(solution)/shard_map/ppermute | solution.py:23
  259.6 7.6 %collective-permute-start.24 = (bf16[4,2688]{1,0:T(4,128)(2,1)S(1)}, bf16[4,2688]{1,0:T(4,128)(2,1)S(1)}, u32[]{:S(2)}, u32[]{:S(2)}) collective-permute-start(bf16[4,2688]{1,0:T(4,128)(2,1)S(1)} %fusion.23), channel_id=1, source_target_pairs={{0,15},{1,0},{2,1},{3,2},{4,3},{5,4},{6,5},{7,6},{8,7},{9,8},{10,9... | collective-permute-start | bytes 64520 | tf_op jit(solution)/shard_map/ppermute | solution.py:25
  262.4 5.9 %collective-permute-start.17 = (bf16[4,2688]{1,0:T(4,128)(2,1)S(1)}, bf16[4,2688]{1,0:T(4,128)(2,1)S(1)}, u32[]{:S(2)}, u32[]{:S(2)}) collective-permute-start(bf16[4,2688]{1,0:T(4,128)(2,1)S(1)} %collective-permute-done.16), channel_id=1, source_target_pairs={{0,1},{1,2},{2,3},{3,4},{4,5},{5,6},{6,7},{7,8},{8,9},{9,10},{10,1... | collective-permute-start | bytes 64520 | tf_op jit(solution)/shard_map/ppermute | solution.py:23
  267.2 7.2 %collective-permute-start.25 = (bf16[4,2688]{1,0:T(4,128)(2,1)S(1)}, bf16[4,2688]{1,0:T(4,128)(2,1)S(1)}, u32[]{:S(2)}, u32[]{:S(2)}) collective-permute-start(bf16[4,2688]{1,0:T(4,128)(2,1)S(1)} %collective-permute-done.24), channel_id=1, source_target_pairs={{0,15},{1,0},{2,1},{3,2},{4,3},{5,4},{6,5},{7,6},{8,7},{9,8},{10,9... | collective-permute-start | bytes 64520 | tf_op jit(solution)/shard_map/ppermute | solution.py:25
  268.3 6.2 %collective-permute-start.18 = (bf16[4,2688]{1,0:T(4,128)(2,1)S(1)}, bf16[4,2688]{1,0:T(4,128)(2,1)S(1)}, u32[]{:S(2)}, u32[]{:S(2)}) collective-permute-start(bf16[4,2688]{1,0:T(4,128)(2,1)S(1)} %collective-permute-done.17), channel_id=1, source_target_pairs={{0,1},{1,2},{2,3},{3,4},{4,5},{5,6},{6,7},{7,8},{8,9},{9,10},{10,1... | collective-permute-start | bytes 64520 | tf_op jit(solution)/shard_map/ppermute | solution.py:23
  274.4 4.0 collective-permute-start.26
  274.6 5.9 %collective-permute-start.19 = (bf16[4,2688]{1,0:T(4,128)(2,1)S(1)}, bf16[4,2688]{1,0:T(4,128)(2,1)S(1)}, u32[]{:S(2)}, u32[]{:S(2)}) collective-permute-start(bf16[4,2688]{1,0:T(4,128)(2,1)S(1)} %collective-permute-done.18), channel_id=1, source_target_pairs={{0,1},{1,2},{2,3},{3,4},{4,5},{5,6},{6,7},{7,8},{8,9},{9,10},{10,1... | collective-permute-start | bytes 64520 | tf_op jit(solution)/shard_map/ppermute | solution.py:23
  278.4 4.1 %collective-permute-start.27 = (bf16[4,2688]{1,0:T(4,128)(2,1)S(1)}, bf16[4,2688]{1,0:T(4,128)(2,1)S(1)}, u32[]{:S(2)}, u32[]{:S(2)}) collective-permute-start(bf16[4,2688]{1,0:T(4,128)(2,1)S(1)} %collective-permute-done.26), channel_id=1, source_target_pairs={{0,15},{1,0},{2,1},{3,2},{4,3},{5,4},{6,5},{7,6},{8,7},{9,8},{10,9... | collective-permute-start | bytes 64520 | tf_op jit(solution)/shard_map/ppermute | solution.py:25
  280.5 5.9 %collective-permute-start.20 = (bf16[4,2688]{1,0:T(4,128)(2,1)S(1)}, bf16[4,2688]{1,0:T(4,128)(2,1)S(1)}, u32[]{:S(2)}, u32[]{:S(2)}) collective-permute-start(bf16[4,2688]{1,0:T(4,128)(2,1)S(1)} %collective-permute-done.19), channel_id=1, source_target_pairs={{0,1},{1,2},{2,3},{3,4},{4,5},{5,6},{6,7},{7,8},{8,9},{9,10},{10,1... | collective-permute-start | bytes 64520 | tf_op jit(solution)/shard_map/ppermute | solution.py:23
  282.5 5.3 %collective-permute-start.28 = (bf16[4,2688]{1,0:T(4,128)(2,1)S(1)}, bf16[4,2688]{1,0:T(4,128)(2,1)S(1)}, u32[]{:S(2)}, u32[]{:S(2)}) collective-permute-start(bf16[4,2688]{1,0:T(4,128)(2,1)S(1)} %collective-permute-done.27), channel_id=1, source_target_pairs={{0,15},{1,0},{2,1},{3,2},{4,3},{5,4},{6,5},{7,6},{8,7},{9,8},{10,9... | collective-permute-start | bytes 64520 | tf_op jit(solution)/shard_map/ppermute | solution.py:25
  286.4 5.9 %collective-permute-start.21 = (bf16[4,2688]{1,0:T(4,128)(2,1)S(1)}, bf16[4,2688]{1,0:T(4,128)(2,1)S(1)}, u32[]{:S(2)}, u32[]{:S(2)}) collective-permute-start(bf16[4,2688]{1,0:T(4,128)(2,1)S(1)} %collective-permute-done.20), channel_id=1, source_target_pairs={{0,1},{1,2},{2,3},{3,4},{4,5},{5,6},{6,7},{7,8},{8,9},{9,10},{10,1... | collective-permute-start | bytes 64520 | tf_op jit(solution)/shard_map/ppermute | solution.py:23
  287.8 5.9 %collective-permute-start.29 = (bf16[4,2688]{1,0:T(4,128)(2,1)S(1)}, bf16[4,2688]{1,0:T(4,128)(2,1)S(1)}, u32[]{:S(2)}, u32[]{:S(2)}) collective-permute-start(bf16[4,2688]{1,0:T(4,128)(2,1)S(1)} %collective-permute-done.28), channel_id=1, source_target_pairs={{0,15},{1,0},{2,1},{3,2},{4,3},{5,4},{6,5},{7,6},{8,7},{9,8},{10,9... | collective-permute-start | bytes 64520 | tf_op jit(solution)/shard_map/ppermute | solution.py:25
  292.3 5.9 %collective-permute-start.22 = (bf16[4,2688]{1,0:T(4,128)(2,1)S(1)}, bf16[4,2688]{1,0:T(4,128)(2,1)S(1)}, u32[]{:S(2)}, u32[]{:S(2)}) collective-permute-start(bf16[4,2688]{1,0:T(4,128)(2,1)S(1)} %collective-permute-done.21), channel_id=1, source_target_pairs={{0,1},{1,2},{2,3},{3,4},{4,5},{5,6},{6,7},{7,8},{8,9},{9,10},{10,1... | collective-permute-start | bytes 64520 | tf_op jit(solution)/shard_map/ppermute | solution.py:23
  293.7 5.9 %collective-permute-start.30 = (bf16[4,2688]{1,0:T(4,128)(2,1)S(1)}, bf16[4,2688]{1,0:T(4,128)(2,1)S(1)}, u32[]{:S(2)}, u32[]{:S(2)}) collective-permute-start(bf16[4,2688]{1,0:T(4,128)(2,1)S(1)} %collective-permute-done.29), channel_id=1, source_target_pairs={{0,15},{1,0},{2,1},{3,2},{4,3},{5,4},{6,5},{7,6},{8,7},{9,8},{10,9... | collective-permute-start | bytes 64520 | tf_op jit(solution)/shard_map/ppermute | solution.py:25
  298.2 5.9 %collective-permute-start.23 = (bf16[4,2688]{1,0:T(4,128)(2,1)S(1)}, bf16[4,2688]{1,0:T(4,128)(2,1)S(1)}, u32[]{:S(2)}, u32[]{:S(2)}) collective-permute-start(bf16[4,2688]{1,0:T(4,128)(2,1)S(1)} %collective-permute-done.22), channel_id=1, source_target_pairs={{0,1},{1,2},{2,3},{3,4},{4,5},{5,6},{6,7},{7,8},{8,9},{9,10},{10,1... | collective-permute-start | bytes 64520 | tf_op jit(solution)/shard_map/ppermute | solution.py:23
Sparse Core Ops, SparseCore 0:
  10.3 136.2 all-gather.1
